TPU v7x, 32 devices: a whole 2x2x4 slice. The times are simulated.
32 devices in a mesh: fsdp: 8 (over z, y), dp: 4 (over x, core).
Axes of the slice: x: 2, y: 2, z: 4, core: 2. Of those that a mesh axis runs over, the one named last changes fastest.
Arguments:
- tokens: bfloat16 [32768, 768], P(('fsdp', 'dp')), may hold values from -6 to 6
- image_table: int32 [160, 3], P(('fsdp', 'dp')), may hold values from 0 to 996, as said below
- ln1_gain: bfloat16 [768], P('fsdp'), may hold values from 0.5 to 1.5
- ln1_bias: bfloat16 [768], P('fsdp'), may hold values from -3 to 3
- qkv_weight: bfloat16 [768, 2304], P('fsdp'), may hold values from -0.21875 to 0.21875
- qkv_bias: bfloat16 [2304], P('fsdp'), may hold values from -2 to 2
- out_weight: bfloat16 [768, 768], P('fsdp'), may hold values from -0.875 to 0.875
- out_bias: bfloat16 [768], P('fsdp'), may hold values from -2 to 2
- ln2_gain: bfloat16 [768], P('fsdp'), may hold values from 0.5 to 1.5
- ln2_bias: bfloat16 [768], P('fsdp'), may hold values from -3 to 3
- fc1_weight: bfloat16 [768, 3072], P('fsdp'), may hold values from -0.21875 to 0.21875
- fc1_bias: bfloat16 [3072], P('fsdp'), may hold values from -3 to 3
- fc2_weight: bfloat16 [3072, 768], P('fsdp'), may hold values from -0.109375 to 0.109375
- fc2_bias: bfloat16 [768], P('fsdp'), may hold values from -2 to 2
- frequencies: bfloat16 [768], P('fsdp'), may hold values from -0.796875 to 0.796875
- cotangent: bfloat16 [32768, 768], P(('fsdp', 'dp')), may hold values from -6 to 6
Outputs:
- block_out: bfloat16 [32768, 768], P(('fsdp', 'dp'))
- tokens_grad: bfloat16 [32768, 768], P(('fsdp', 'dp'))
- first_norm_gain_gradient: float32 [768], P('fsdp')
- ln1_bias_grad: float32 [768], P('fsdp')
- qkv_weight_grad: float32 [768, 2304], P('fsdp')
- qkv_bias_grad: float32 [2304], P('fsdp')
- out_weight_grad: float32 [768, 768], P('fsdp')
- out_bias_grad: float32 [768], P('fsdp')
- second_norm_gain_gradient: float32 [768], P('fsdp')
- ln2_bias_grad: float32 [768], P('fsdp')
- fc1_weight_grad: float32 [768, 3072], P('fsdp')
- fc1_bias_grad: float32 [3072], P('fsdp')
- fc2_weight_grad: float32 [3072, 768], P('fsdp')
- fc2_bias_grad: float32 [768], P('fsdp')
- frequencies_grad: float32 [768], P('fsdp')
- freq_grad_norm: float32 [], replicated
- other_grad_norm: float32 [], replicated
Inputs may be any that keep to these rules, and one draw needn't show every extreme that they name: `image_table`: rows 5b to 5b+4 describe bin b: either a 24x24 and a 20x20 image, or 24x24 and two 14x14, or two 20x20 and one 14x14, or one 20x20 and three 14x14, or five 14x14, laid end to end from offset 0 in the listed order; unused rows have height and width 0 and the offset where the used rows end. Grids are square.
All inputs are finite; a program needn't handle non-finite values.
Results may differ from a plain program's by a relative error of at most 0.015.
Values may be sent and summed in bfloat16 or wider, within the bound.
No kernel may reach another device: no remote copies, remote signals or barrier semaphores. Data moves between devices by JAX's collectives and lax.ppermute only.
A program may use at most 192 MiB of HBM per device.

v0:
```python
import jax
import jax.numpy as jnp
from jax import lax
from jax.sharding import PartitionSpec as P

H = 12
HD = 64
BIN = 1024
norm_eps = 1e-06
masked_score = -1e30
inv_sqrt_two_pi = 0.3989422804014327


def matmul(left, right):
    return jnp.dot(left, right, preferred_element_type=jnp.float32)


def matmul_left_t(left, right):
    return lax.dot_general(
        left, right, (((0,), (0,)), ((), ())), preferred_element_type=jnp.float32
    )


def matmul_right_t(left, right):
    return lax.dot_general(
        left, right, (((1,), (1,)), ((), ())), preferred_element_type=jnp.float32
    )


def image_layout(image_table, bin_count, bin_rows):
    slot_count = image_table.shape[0] // bin_count
    table = image_table.reshape(bin_count, slot_count, 3)
    offset = table[:, :, 0:1]
    height = table[:, :, 1:2]
    width = table[:, :, 2:3]
    place = jnp.arange(bin_rows, dtype=jnp.int32)[None, None, :]
    inside = ((place >= offset) & (place < offset + height * width)).astype(jnp.int32)
    live = jnp.sum(inside, axis=1)
    slot_ids = jnp.arange(slot_count, dtype=jnp.int32)[None, :, None]
    segment = jnp.sum(inside * slot_ids, axis=1) + slot_count * (1 - live)
    local_place = place[:, 0, :] - jnp.sum(inside * offset, axis=1)
    grid_width = jnp.maximum(jnp.sum(inside * width, axis=1), 1)
    grid_row = local_place // grid_width * live
    grid_col = local_place % grid_width * live
    return (
        segment,
        grid_row.reshape(-1).astype(jnp.float32),
        grid_col.reshape(-1).astype(jnp.float32),
    )


def rotary_tables(frequencies, grid_row, grid_col):
    half_width = frequencies.shape[0] // 2
    freq_float = frequencies.astype(jnp.float32)
    freq_row = freq_float[:half_width].reshape(H, HD // 2)
    freq_col = freq_float[half_width:].reshape(H, HD // 2)
    theta = grid_row[:, None, None] * freq_row[None] + grid_col[:, None, None] * freq_col[None]
    return (jnp.cos(theta), jnp.sin(theta))


def rotate(heads, cosine, sine):
    half_width = heads.shape[-1] // 2
    first = heads[..., :half_width]
    second = heads[..., half_width:]
    return jnp.concatenate(
        [first * cosine - second * sine, first * sine + second * cosine], axis=-1
    )


def layer_norm_forward(values):
    center = values - jnp.mean(values, axis=-1, keepdims=True)
    inverse_deviation = lax.rsqrt(jnp.mean(center * center, axis=-1, keepdims=True) + norm_eps)
    return (center * inverse_deviation, inverse_deviation)


def layer_norm_backward(
    gradient_norm_total, centered_normalized, inverse_deviation, norm_gain_vector
):
    gain_scaled_output = gradient_norm_total * norm_gain_vector
    return inverse_deviation * (
        gain_scaled_output
        - jnp.mean(gain_scaled_output, axis=-1, keepdims=True)
        - centered_normalized
        * jnp.mean(gain_scaled_output * centered_normalized, axis=-1, keepdims=True)
    )


def gelu_slope(values):
    return (
        0.5 * (1.0 + lax.erf(values * 0.7071067811865476))
        + values * jnp.exp(-0.5 * values * values) * inv_sqrt_two_pi
    )


def join_heads(stacked):
    return jnp.transpose(stacked, (1, 0, 2)).reshape(stacked.shape[1], H * HD)


def head_slice(matrix, head_index):
    return lax.dynamic_slice_in_dim(matrix, head_index * HD, HD, 1)


def attend_bin(packed):
    query, key_rows, value, segment = packed
    mask = segment[:, None] == segment[None, :]
    scale = HD ** (-0.5)

    def one_head(head_index):
        q_head = head_slice(query, head_index)
        k_head = head_slice(key_rows, head_index)
        v_head = head_slice(value, head_index)
        scores = jnp.where(mask, matmul_right_t(q_head, k_head) * scale, masked_score)
        top = jnp.max(scores, axis=-1, keepdims=True)
        log_total = top + jnp.log(jnp.sum(jnp.exp(scores - top), axis=-1, keepdims=True))
        probs = jnp.exp(scores - log_total).astype(jnp.bfloat16)
        return (matmul(probs, v_head).astype(jnp.bfloat16), log_total[:, 0])

    mixed, log_total = lax.map(one_head, jnp.arange(H, dtype=jnp.int32))
    return (join_heads(mixed), log_total)


def attend_bin_back(packed):
    query, key_rows, value, d_mixed, log_total, segment = packed
    mask = segment[:, None] == segment[None, :]
    scale = HD ** (-0.5)

    def one_head(head_index):
        q_head = head_slice(query, head_index)
        k_head = head_slice(key_rows, head_index)
        v_head = head_slice(value, head_index)
        d_head = head_slice(d_mixed, head_index)
        total_head = lax.dynamic_index_in_dim(log_total, head_index, 0, keepdims=False)
        scores = jnp.where(mask, matmul_right_t(q_head, k_head) * scale, masked_score)
        probs = jnp.exp(scores - total_head[:, None])
        d_probs = matmul_right_t(d_head, v_head)
        d_value = matmul_left_t(probs.astype(jnp.bfloat16), d_head)
        inner = jnp.sum(probs * d_probs, axis=-1, keepdims=True)
        d_scores = (probs * (d_probs - inner)).astype(jnp.bfloat16)
        d_query = matmul(d_scores, k_head) * scale
        d_key = matmul_left_t(d_scores, q_head) * scale
        return (d_query, d_key, d_value)

    d_query, d_key, d_value = lax.map(one_head, jnp.arange(H, dtype=jnp.int32))
    return (join_heads(d_query), join_heads(d_key), join_heads(d_value))


def square_sums(pieces):
    freq_sq = jnp.sum(pieces[12] * pieces[12])
    other_sq = jnp.float32(0.0)
    for member in pieces[:12]:
        other_sq = other_sq + jnp.sum(member * member)
    return (freq_sq, other_sq)


def shards(
    tokens,
    image_table,
    ln1_gain,
    ln1_bias,
    qkv_weight,
    qkv_bias,
    out_weight,
    out_bias,
    ln2_gain,
    ln2_bias,
    fc1_weight,
    fc1_bias,
    fc2_weight,
    fc2_bias,
    frequencies,
    cotangent,
):
    block_parameters = (
        lax.all_gather(ln1_gain, "fsdp", axis=0, tiled=True),
        lax.all_gather(ln1_bias, "fsdp", axis=0, tiled=True),
        lax.all_gather(qkv_weight, "fsdp", axis=0, tiled=True),
        lax.all_gather(qkv_bias, "fsdp", axis=0, tiled=True),
        lax.all_gather(out_weight, "fsdp", axis=0, tiled=True),
        lax.all_gather(out_bias, "fsdp", axis=0, tiled=True),
        lax.all_gather(ln2_gain, "fsdp", axis=0, tiled=True),
        lax.all_gather(ln2_bias, "fsdp", axis=0, tiled=True),
        lax.all_gather(fc1_weight, "fsdp", axis=0, tiled=True),
        lax.all_gather(fc1_bias, "fsdp", axis=0, tiled=True),
        lax.all_gather(fc2_weight, "fsdp", axis=0, tiled=True),
        lax.all_gather(fc2_bias, "fsdp", axis=0, tiled=True),
        lax.all_gather(frequencies, "fsdp", axis=0, tiled=True),
    )
    row_count, width = tokens.shape
    bin_count = row_count // BIN
    half_head = HD // 2
    segment, grid_row, grid_col = image_layout(image_table, bin_count, BIN)
    cosine, sine = rotary_tables(block_parameters[12], grid_row, grid_col)
    input_single_precision = tokens.astype(jnp.float32)
    first_centered_normalized, first_inverse_deviation = layer_norm_forward(input_single_precision)
    first_activation = (
        first_centered_normalized * block_parameters[0].astype(jnp.float32)
        + block_parameters[1].astype(jnp.float32)
    ).astype(jnp.bfloat16)
    qkv_full = matmul(first_activation, block_parameters[2]) + block_parameters[3].astype(
        jnp.float32
    )
    q_rot = rotate(qkv_full[:, :width].reshape(row_count, H, HD), cosine, sine)
    k_rot = rotate(qkv_full[:, width : 2 * width].reshape(row_count, H, HD), cosine, sine)
    q_low = q_rot.reshape(row_count, width).astype(jnp.bfloat16)
    k_low = k_rot.reshape(row_count, width).astype(jnp.bfloat16)
    v_low = qkv_full[:, 2 * width :].astype(jnp.bfloat16)
    q_bins = q_low.reshape(bin_count, BIN, width)
    k_bins = k_low.reshape(bin_count, BIN, width)
    v_bins = v_low.reshape(bin_count, BIN, width)
    mixed, log_total = lax.map(attend_bin, (q_bins, k_bins, v_bins, segment))
    mixed = mixed.reshape(row_count, width)
    residual_stream = (
        input_single_precision
        + matmul(mixed, block_parameters[4])
        + block_parameters[5].astype(jnp.float32)
    )
    second_centered_normalized, second_inverse_deviation = layer_norm_forward(residual_stream)
    second_activation = (
        second_centered_normalized * block_parameters[6].astype(jnp.float32)
        + block_parameters[7].astype(jnp.float32)
    ).astype(jnp.bfloat16)
    up_proj = matmul(second_activation, block_parameters[8]) + block_parameters[9].astype(
        jnp.float32
    )
    gelu_low = jax.nn.gelu(up_proj, approximate=False).astype(jnp.bfloat16)
    block_out = (
        residual_stream
        + matmul(gelu_low, block_parameters[10])
        + block_parameters[11].astype(jnp.float32)
    ).astype(jnp.bfloat16)
    block_parameters = (
        lax.all_gather(ln1_gain, "fsdp", axis=0, tiled=True),
        lax.all_gather(ln1_bias, "fsdp", axis=0, tiled=True),
        lax.all_gather(qkv_weight, "fsdp", axis=0, tiled=True),
        lax.all_gather(qkv_bias, "fsdp", axis=0, tiled=True),
        lax.all_gather(out_weight, "fsdp", axis=0, tiled=True),
        lax.all_gather(out_bias, "fsdp", axis=0, tiled=True),
        lax.all_gather(ln2_gain, "fsdp", axis=0, tiled=True),
        lax.all_gather(ln2_bias, "fsdp", axis=0, tiled=True),
        lax.all_gather(fc1_weight, "fsdp", axis=0, tiled=True),
        lax.all_gather(fc1_bias, "fsdp", axis=0, tiled=True),
        lax.all_gather(fc2_weight, "fsdp", axis=0, tiled=True),
        lax.all_gather(fc2_bias, "fsdp", axis=0, tiled=True),
        lax.all_gather(frequencies, "fsdp", axis=0, tiled=True),
    )
    output_gradient = cotangent.astype(jnp.float32)
    fc2_bias_grad = jnp.sum(output_gradient, axis=0)
    fc2_weight_grad = matmul_left_t(gelu_low, cotangent)
    d_up = (matmul_right_t(cotangent, block_parameters[10]) * gelu_slope(up_proj)).astype(
        jnp.bfloat16
    )
    fc1_bias_grad = jnp.sum(d_up.astype(jnp.float32), axis=0)
    fc1_weight_grad = matmul_left_t(second_activation, d_up)
    second_activation_gradient = matmul_right_t(d_up, block_parameters[8])
    second_norm_gain_gradient = jnp.sum(
        second_activation_gradient * second_centered_normalized, axis=0
    )
    ln2_bias_grad = jnp.sum(second_activation_gradient, axis=0)
    residual_gradient = output_gradient + layer_norm_backward(
        second_activation_gradient,
        second_centered_normalized,
        second_inverse_deviation,
        block_parameters[6].astype(jnp.float32),
    )
    d_att = residual_gradient.astype(jnp.bfloat16)
    out_bias_grad = jnp.sum(d_att.astype(jnp.float32), axis=0)
    out_weight_grad = matmul_left_t(mixed, d_att)
    d_mixed = matmul_right_t(d_att, block_parameters[4]).astype(jnp.bfloat16)
    d_qrot, d_krot, d_value = lax.map(
        attend_bin_back,
        (q_bins, k_bins, v_bins, d_mixed.reshape(bin_count, BIN, width), log_total, segment),
    )
    d_qrot = d_qrot.reshape(row_count, H, HD)
    d_krot = d_krot.reshape(row_count, H, HD)
    d_theta = (
        d_qrot[..., half_head:] * q_rot[..., :half_head]
        - d_qrot[..., :half_head] * q_rot[..., half_head:]
    )
    d_theta = (
        d_theta
        + d_krot[..., half_head:] * k_rot[..., :half_head]
        - d_krot[..., :half_head] * k_rot[..., half_head:]
    )
    frequencies_grad = jnp.concatenate(
        [
            jnp.sum(grid_row[:, None, None] * d_theta, axis=0).reshape(-1),
            jnp.sum(grid_col[:, None, None] * d_theta, axis=0).reshape(-1),
        ]
    )
    d_query = rotate(d_qrot, cosine, -sine).reshape(row_count, width)
    d_key = rotate(d_krot, cosine, -sine).reshape(row_count, width)
    d_qkv = jnp.concatenate([d_query, d_key, d_value.reshape(row_count, width)], axis=1).astype(
        jnp.bfloat16
    )
    qkv_bias_grad = jnp.sum(d_qkv.astype(jnp.float32), axis=0)
    qkv_weight_grad = matmul_left_t(first_activation, d_qkv)
    first_activation_gradient = matmul_right_t(d_qkv, block_parameters[2])
    first_norm_gain_gradient = jnp.sum(
        first_activation_gradient * first_centered_normalized, axis=0
    )
    ln1_bias_grad = jnp.sum(first_activation_gradient, axis=0)
    tokens_grad = (
        residual_gradient
        + layer_norm_backward(
            first_activation_gradient,
            first_centered_normalized,
            first_inverse_deviation,
            block_parameters[0].astype(jnp.float32),
        )
    ).astype(jnp.bfloat16)
    pieces = (
        lax.psum_scatter(first_norm_gain_gradient, "fsdp", scatter_dimension=0, tiled=True),
        lax.psum_scatter(ln1_bias_grad, "fsdp", scatter_dimension=0, tiled=True),
        lax.psum_scatter(qkv_weight_grad, "fsdp", scatter_dimension=0, tiled=True),
        lax.psum_scatter(qkv_bias_grad, "fsdp", scatter_dimension=0, tiled=True),
        lax.psum_scatter(out_weight_grad, "fsdp", scatter_dimension=0, tiled=True),
        lax.psum_scatter(out_bias_grad, "fsdp", scatter_dimension=0, tiled=True),
        lax.psum_scatter(second_norm_gain_gradient, "fsdp", scatter_dimension=0, tiled=True),
        lax.psum_scatter(ln2_bias_grad, "fsdp", scatter_dimension=0, tiled=True),
        lax.psum_scatter(fc1_weight_grad, "fsdp", scatter_dimension=0, tiled=True),
        lax.psum_scatter(fc1_bias_grad, "fsdp", scatter_dimension=0, tiled=True),
        lax.psum_scatter(fc2_weight_grad, "fsdp", scatter_dimension=0, tiled=True),
        lax.psum_scatter(fc2_bias_grad, "fsdp", scatter_dimension=0, tiled=True),
        lax.psum_scatter(frequencies_grad, "fsdp", scatter_dimension=0, tiled=True),
    )
    pieces = (
        lax.psum(pieces[0].astype(jnp.bfloat16), "dp").astype(jnp.float32),
        lax.psum(pieces[1].astype(jnp.bfloat16), "dp").astype(jnp.float32),
        lax.psum(pieces[2].astype(jnp.bfloat16), "dp").astype(jnp.float32),
        lax.psum(pieces[3].astype(jnp.bfloat16), "dp").astype(jnp.float32),
        lax.psum(pieces[4].astype(jnp.bfloat16), "dp").astype(jnp.float32),
        lax.psum(pieces[5].astype(jnp.bfloat16), "dp").astype(jnp.float32),
        lax.psum(pieces[6].astype(jnp.bfloat16), "dp").astype(jnp.float32),
        lax.psum(pieces[7].astype(jnp.bfloat16), "dp").astype(jnp.float32),
        lax.psum(pieces[8].astype(jnp.bfloat16), "dp").astype(jnp.float32),
        lax.psum(pieces[9].astype(jnp.bfloat16), "dp").astype(jnp.float32),
        lax.psum(pieces[10].astype(jnp.bfloat16), "dp").astype(jnp.float32),
        lax.psum(pieces[11].astype(jnp.bfloat16), "dp").astype(jnp.float32),
        lax.psum(pieces[12].astype(jnp.bfloat16), "dp").astype(jnp.float32),
    )
    freq_sq, other_sq = square_sums(pieces)
    freq_sq, other_sq = lax.psum((freq_sq, other_sq), "fsdp")
    return (
        block_out,
        tokens_grad,
        pieces[0],
        pieces[1],
        pieces[2],
        pieces[3],
        pieces[4],
        pieces[5],
        pieces[6],
        pieces[7],
        pieces[8],
        pieces[9],
        pieces[10],
        pieces[11],
        pieces[12],
        jnp.sqrt(freq_sq),
        jnp.sqrt(other_sq),
    )


def solution(mesh):
    placed = (
        P(("fsdp", "dp"), None),
        P(("fsdp", "dp"), None),
        P("fsdp"),
        P("fsdp"),
        P("fsdp", None),
        P("fsdp"),
        P("fsdp", None),
        P("fsdp"),
        P("fsdp"),
        P("fsdp"),
        P("fsdp", None),
        P("fsdp"),
        P("fsdp", None),
        P("fsdp"),
        P("fsdp"),
        P(("fsdp", "dp"), None),
    )
    return jax.shard_map(
        shards,
        mesh=mesh,
        in_specs=placed,
        out_specs=(
            P(("fsdp", "dp"), None),
            P(("fsdp", "dp"), None),
            P("fsdp"),
            P("fsdp"),
            P("fsdp", None),
            P("fsdp"),
            P("fsdp", None),
            P("fsdp"),
            P("fsdp"),
            P("fsdp"),
            P("fsdp", None),
            P("fsdp"),
            P("fsdp", None),
            P("fsdp"),
            P("fsdp"),
            P(),
            P(),
        ),
        check_vma=False,
    )
```

profile of v0, /device:TPU:0, one launch (start us, length us, event | category | flops | bytes accessed | tf_op | source)
XLA Modules:
  0.0 1132.7 jit_solution(17472799987714436141)
XLA Ops:
  19.5 40.6 %all-reduce.19 = (bf16[768]{0:T(1024)(128)(2,1)S(1)}, bf16[2304]{0:T(1024)(128)(2,1)S(1)}, bf16[768]{0:T(1024)(128)(2,1)S(1)}, bf16[768]{0:T(1024)(128)(2,1)S(1)...) all-reduce(bf16[768]{0:T(1024)(128)(2,1)S(1)} %dynamic-update-slice, ...), channel_id=1, replica_groups=mesh['fsdp'=8,'dp'=4] {'fsdp'}, use_global_device_ids=true, to_apply=%add.3 | all-reduce | flops 7680 | bytes 30720
  62.9 26.9 %all-gather = bf16[8,1,384]{2,1,0:T(2,128)(2,1)S(1)} all-gather(bf16[1,1,384]{2,1,0:T(2,128)(2,1)S(1)} %reshape.697), channel_id=1, replica_groups=mesh['fsdp'=8,'dp'=4] {'fsdp'}, dimensions={0}, use_global_device_ids=true | all-gather | bytes 6912 | tf_op jit(solution)/shard_map/all_gather | solution.py:183
  91.9 6.3 convolution_add_fusion
  98.2 3.0 fusion.95
  102.6 3.6 copy.82
  106.1 3.5 copy.81
  109.7 10.8 fusion.87
  126.9 83.8 %while.48 = (s32[]{:T(128)}, bf16[12,1024,64]{1,2,0:T(8,128)(2,1)}, f32[12,1024]{1,0:T(8,128)S(1)}, s32[12]{0:T(128)S(1)}, bf16[1024,768]{1,0:T(8,128)(2,1)S(1)}...) while((s32[]{:T(128)}, bf16[12,1024,64]{1,2,0:T(8,128)(2,1)}, ...), condition=%wide.region_9.10_spmd.clone, body=%wide.region_6.9_spmd.clone.sunk | while | flops 283180032 | bytes 13558979 | solution.py:118
  145.0 2.8 fusion.137
  158.9 2.8 fusion.137
  165.9 2.8 fusion.137
  172.9 2.8 fusion.137
  207.8 2.8 fusion.137
  210.8 3.9 fusion.98
  216.8 50.6 %fusion.44 = (bf16[1024,3072]{1,0:T(8,128)(2,1)}, f32[1024,3072]{1,0:T(8,128)}) fusion(f32[3072]{0:T(1024)S(1)} %bitcast.103, bf16[768,3072]{1,0:T(8,128)(2,1)} %all-gather.10.cloned.1.call-done, f32[1024,768]{0,1:T(8,128)} %copy-done.4, f32[768]{0:T(1024)S(1)} %convert_element_type.206, f32[768]{0:T(1024)S(1)} %convert_element_type.205, ...), kind=kOutput, calls=%fused_computation.50 | convolution fusion | flops 5043388416 | bytes 26765312 | tf_op jit(solution)/shard_map/dot_general | solution.py:15
  267.4 13.0 %all-gather.12.cloned.1.call-done = bf16[3072,768]{1,0:T(8,128)(2,1)} async-done(((bf16[384,768]{1,0:T(8,128)(2,1)}), bf16[3072,768]{1,0:T(8,128)(2,1)}) %all-gather.12.cloned.1.call-update) | async-done | bytes 4718608 | tf_op jit(solution)/shard_map/all_gather | solution.py:184
  280.4 11.9 %convert_reduce_fusion = (f32[3072]{0:T(1024)S(1)}, bf16[1024,3072]{1,0:T(8,128)(2,1)S(1)}) fusion(f32[1024,3072]{1,0:T(8,128)} %get-tuple-element.504, f32[3072]{0:T(1024)S(1)} %bitcast.104, bf16[1024,768]{1,0:T(8,128)(2,1)S(1)} %copy-done.15, bf16[3072,768]{1,0:T(8,128)(2,1)} %all-gather.12.cloned.1.call-done), kind=kOutput, calls=%fused_computation.57 | convolution fusion | flops 4872729600 | bytes 25190400 | tf_op jit(solution)/shard_map/dot_general | solution.py:25
  292.3 6.7 fusion.100
  299.1 3.7 copy.87
  302.8 3.0 multiply_reduce_fusion.1
  312.6 4.5 convolution_convert_fusion
  317.1 230.8 %while.49 = (s32[]{:T(128)}, f32[12,1024,64]{1,2,0:T(8,128)}, f32[12,1024,64]{1,2,0:T(8,128)}, bf16[12,1024,64]{1,2,0:T(8,128)(2,1)}, s32[12]{0:T(128)S(1)}, /*i...) while((s32[]{:T(128)}, f32[12,1024,64]{1,2,0:T(8,128)}, ...), condition=%wide.region_16.17_spmd.clone, body=%wide.region_14.16_spmd.clone.sunk | while | flops 681704448 | bytes 50886960 | solution.py:143
  318.9 3.8 fusion.146
  324.6 3.9 multiply_reduce_fusion.22
  338.1 3.8 fusion.146
  343.8 3.9 multiply_reduce_fusion.22
  357.3 3.8 fusion.146
  363.0 3.9 multiply_reduce_fusion.22
  376.5 3.8 fusion.146
  382.2 3.9 multiply_reduce_fusion.22
  395.7 3.8 fusion.146
  401.4 3.9 multiply_reduce_fusion.22
  414.9 3.8 fusion.146
  420.6 3.9 multiply_reduce_fusion.22
  434.1 3.8 fusion.146
  439.8 3.9 multiply_reduce_fusion.22
  453.3 3.8 fusion.146
  459.0 3.9 multiply_reduce_fusion.22
  472.4 3.8 fusion.146
  478.2 3.9 multiply_reduce_fusion.22
  491.6 3.8 fusion.146
  497.3 3.9 multiply_reduce_fusion.22
  510.8 3.8 fusion.146
  516.5 3.9 multiply_reduce_fusion.22
  529.9 3.8 fusion.146
  535.7 3.9 multiply_reduce_fusion.22
  547.9 12.2 %multiply_subtract_fusion = (f32[1024,12,32]{0,2,1:T(8,128)S(1)}, bf16[1024,12,32]{0,2,1:T(8,128)(2,1)S(1)}, bf16[1024,12,32]{0,2,1:T(8,128)(2,1)S(1)}, bf16[1024,12,32]{0,2,1:T(8,128)(2,1)S(1)}) fusion(f32[1024,12,64]{0,2,1:T(8,128)} %bitcast.87, f32[1024,12,64]{0,2,1:T(8,128)} %bitcast.97, f32[1024,12,64]{0,2,1:T(8,128)} %bitcast.86, ...), kind=kLoop, calls=%fused_computation.114 | loop fusion | flops 13762560 | bytes 16526336 | tf_op jit(solution)/shard_map/sub | solution.py:280
  560.2 6.4 multiply_reduce_fusion.7
  569.1 7.0 fusion.89
  576.2 10.6 fusion.93
  586.8 9.9 fusion.101
  599.3 10.1 add_convert_fusion
  612.1 8.6 fusion.99
  620.7 3.5 copy.90
  624.2 3.1 fusion.71
  627.3 4.1 fusion.70
  636.2 35.3 %all-reduce.18 = (bf16[768]{0:T(1024)(128)(2,1)S(1)}, bf16[768]{0:T(1024)(128)(2,1)S(1)}, bf16[2304]{0:T(1024)(128)(2,1)S(1)}, bf16[768]{0:T(1024)(128)(2,1)S(1)...) all-reduce(f32[768]{0:T(1024)S(1)} %get-tuple-element.365, ...), channel_id=2, replica_groups=mesh['fsdp'=8,'dp'=4] {'fsdp'}, use_global_device_ids=true, to_apply=%region_20.21.clone | all-reduce | flops 10752 | bytes 64512
  672.2 6.1 all-reduce.20
  686.8 18.9 %reduce-scatter.5.cloned.1.call-done = f32[96,2304]{1,0:T(8,128)} async-done(((f32[768,2304]{1,0:T(8,128)}), f32[96,2304]{1,0:T(8,128)}) %reduce-scatter.5.cloned.1.call-update) | async-done | bytes 884752 | tf_op jit(solution)/shard_map/reduce_scatter | solution.py:314
  707.7 162.8 %reduce-scatter.9.cloned.1.call-done = f32[96,3072]{1,0:T(8,128)} async-done(((f32[768,3072]{1,0:T(8,128)}), f32[96,3072]{1,0:T(8,128)}) %reduce-scatter.9.cloned.1.call-update) | async-done | bytes 1179664 | tf_op jit(solution)/shard_map/reduce_scatter | solution.py:320
  872.6 162.7 %reduce-scatter.11.cloned.1.call-done = f32[384,768]{1,0:T(8,128)} async-done(((f32[3072,768]{1,0:T(8,128)}), f32[384,768]{1,0:T(8,128)}) %reduce-scatter.11.cloned.1.call-update) | async-done | bytes 1179664 | tf_op jit(solution)/shard_map/reduce_scatter | solution.py:322
  1042.2 42.1 %all-reduce.24.cloned.1.call-done = (bf16[96,2304]{1,0:T(8,128)(2,1)}, bf16[96,768]{1,0:T(8,128)(2,1)}, bf16[96,3072]{1,0:T(8,128)(2,1)}, bf16[384,768]{1,0:T(8,128)(2,1)}) async-done(((bf16[96,2304]{1,0:T(8,128)(2,1)}, bf16[96,768]{1,0:T(8,128)(2,1)}, bf16[96,3072]{1,0:T(8,128)(2,1)}, bf16[384,768]{1,0:T(8,128)(2,1)}), (bf16[96,2304]{1,0:T(8,128)(2,1)}, bf16[96,768]{1,0:T(8,128)(2,1)}, ...) | async-done | bytes 1769488 | tf_op jit(solution)/shard_map/psum | solution.py:329
  1089.3 3.0 multiply_reduce_fusion.9
  1100.3 22.0 %all-reduce.17 = (f32[]{:T(128)}, f32[]{:T(128)}) all-reduce(f32[]{:T(128)} %get-tuple-element.469, f32[]{:T(128)S(6)} %add.305), channel_id=1, replica_groups=mesh['fsdp'=8,'dp'=4] {'fsdp'}, use_global_device_ids=true, to_apply=%region_56.57 | all-reduce | flops 2 | bytes 16 | tf_op jit(solution)/shard_map/psum | solution.py:342
  (356 shorter events, 236.6 us)
Async XLA Ops:
  7.2 84.7 %all-gather.6.cloned.1.call-start = ((), (), s32[]{:S(2)}) async-start(), calls=%async_computation.4 | async-start | bytes 3981312 | tf_op jit(solution)/shard_map/all_gather | solution.py:176
  7.9 202.8 %all-gather.8.cloned.1.call-start = ((), (), s32[]{:S(2)}) async-start(), calls=%async_computation.5 | async-start | bytes 1327104 | tf_op jit(solution)/shard_map/all_gather | solution.py:178
  8.7 208.1 %all-gather.10.cloned.1.call-start = ((), (), s32[]{:S(2)}) async-start(), calls=%async_computation.6 | async-start | bytes 5308416 | tf_op jit(solution)/shard_map/all_gather | solution.py:182
  9.4 271.0 %all-gather.12.cloned.1.call-start = ((), (), s32[]{:S(2)}) async-start(), calls=%async_computation.7 | async-start | bytes 5308416 | tf_op jit(solution)/shard_map/all_gather | solution.py:184
  10.0 675.2 %reduce-scatter.7.cloned.1.call-start = ((), (), s32[]{:S(2)}) async-start(), calls=%async_computation.9 | async-start | bytes 2654208 | tf_op jit(solution)/shard_map/reduce_scatter | solution.py:316
  60.0 2.8 copy-start.35
  60.0 2.9 copy-start.36
  60.1 29.8 %copy-start.14 = (bf16[1024,768]{1,0:T(8,128)(2,1)S(1)}, bf16[1024,768]{1,0:T(8,128)(2,1)}, u32[]{:S(2)}) copy-start(bf16[1024,768]{1,0:T(8,128)(2,1)} %param.35) | copy-start | bytes 4718596
  61.9 148.8 %copy-start.1 = (bf16[1024,768]{0,1:T(8,128)(2,1)}, bf16[1024,768]{0,1:T(8,128)(2,1)S(1)}, u32[]{:S(2)}) copy-start(bf16[1024,768]{0,1:T(8,128)(2,1)S(1)} %copy.80) | copy-start | bytes 4718596
  61.9 29.9 %copy-start.32 = (f32[768]{0:T(1024)}, f32[768]{0:T(1024)S(1)}, u32[]{:S(2)}) copy-start(f32[768]{0:T(1024)S(1)} %convert_element_type.195) | copy-start | bytes 9220
  62.0 29.9 %copy-start.28 = (f32[768]{0:T(1024)}, f32[768]{0:T(1024)S(1)}, u32[]{:S(2)}) copy-start(f32[768]{0:T(1024)S(1)} %convert_element_type.194) | copy-start | bytes 9220
  62.2 36.0 %copy-start.22 = (f32[1024]{0:T(1024)}, f32[1024]{0:T(1024)S(1)}, u32[]{:S(2)}) copy-start(f32[1024]{0:T(1024)S(1)} %broadcast_multiply_fusion.5) | copy-start | bytes 12292
  62.7 35.5 %copy-start.30 = (f32[1024]{0:T(1024)}, f32[1024]{0:T(1024)S(1)}, u32[]{:S(2)}) copy-start(f32[1024]{0:T(1024)S(1)} %add_rsqrt_fusion.1) | copy-start | bytes 12292
  62.8 46.8 %copy-start.18 = (f32[12,32]{1,0:T(8,128)}, f32[12,32]{1,0:T(8,128)S(1)}, u32[]{:S(2)}) copy-start(f32[12,32]{1,0:T(8,128)S(1)} %slice.81) | copy-start | bytes 4612
  62.9 46.7 %copy-start.20 = (f32[12,32]{1,0:T(8,128)}, f32[12,32]{1,0:T(8,128)S(1)}, u32[]{:S(2)}) copy-start(f32[12,32]{1,0:T(8,128)S(1)} %slice.79) | copy-start | bytes 4612
  91.8 17.8 %copy-start.24 = (f32[1024]{0:T(1024)}, f32[1024]{0:T(1024)S(1)}, u32[]{:S(2)}) copy-start(f32[1024]{0:T(1024)S(1)} %get-tuple-element.490) | copy-start | bytes 12292
  91.8 17.8 %copy-start.26 = (f32[1024]{0:T(1024)}, f32[1024]{0:T(1024)S(1)}, u32[]{:S(2)}) copy-start(f32[1024]{0:T(1024)S(1)} %get-tuple-element.491) | copy-start | bytes 12292
  210.7 4.0 copy-start.10
  214.7 1.7 copy-start.4
  216.8 63.6 %copy-start.15 = (bf16[1024,768]{1,0:T(8,128)(2,1)S(1)}, bf16[1024,768]{1,0:T(8,128)(2,1)}, u32[]{:S(2)}) copy-start(bf16[1024,768]{1,0:T(8,128)(2,1)} %param.35) | copy-start | bytes 4718596
  280.4 11.9 %copy-start.37 = (bf16[768,3072]{1,0:T(8,128)(2,1)S(1)}, bf16[768,3072]{1,0:T(8,128)(2,1)}, u32[]{:S(2)}) copy-start(bf16[768,3072]{1,0:T(8,128)(2,1)} %all-gather.10.cloned.1.call-done) | copy-start | bytes 14155780
  292.3 6.8 copy-start.40
  299.0 3.7 copy-start.5
  302.8 3.1 copy-start.7
  302.8 3.3 copy-start.13
  306.1 3.5 copy-start.39
  307.9 1.7 copy-start.9
  309.5 3.1 copy-start.38
  312.4 393.3 %reduce-scatter.5.cloned.1.call-start = ((), (), s32[]{:S(2)}) async-start(), calls=%async_computation.8 | async-start | bytes 7962624 | tf_op jit(solution)/shard_map/reduce_scatter | solution.py:314
  317.1 230.8 %copy-start.3 = (f32[1024,768]{0,1:T(8,128)S(1)}, f32[1024,768]{0,1:T(8,128)}, u32[]{:S(2)}) copy-start(f32[1024,768]{0,1:T(8,128)} %copy.82) | copy-start | bytes 9437188
  317.1 230.8 %copy-start.19 = (f32[12,32]{1,0:T(8,128)S(1)}, f32[12,32]{1,0:T(8,128)}, u32[]{:S(2)}) copy-start(f32[12,32]{1,0:T(8,128)} %copy-done.18) | copy-start | bytes 4612
  317.1 230.8 %copy-start.21 = (f32[12,32]{1,0:T(8,128)S(1)}, f32[12,32]{1,0:T(8,128)}, u32[]{:S(2)}) copy-start(f32[12,32]{1,0:T(8,128)} %copy-done.20) | copy-start | bytes 4612
  317.1 230.8 %copy-start.25 = (f32[1024]{0:T(1024)S(1)}, f32[1024]{0:T(1024)}, u32[]{:S(2)}) copy-start(f32[1024]{0:T(1024)} %copy-done.24) | copy-start | bytes 12292
  317.1 230.8 %copy-start.27 = (f32[1024]{0:T(1024)S(1)}, f32[1024]{0:T(1024)}, u32[]{:S(2)}) copy-start(f32[1024]{0:T(1024)} %copy-done.26) | copy-start | bytes 12292
  324.6 3.9 copy-start
  343.8 4.0 copy-start
  363.0 3.9 copy-start
  382.2 3.9 copy-start
  401.4 3.9 copy-start
  420.6 3.9 copy-start
  439.8 3.9 copy-start
  459.0 3.9 copy-start
  478.2 3.9 copy-start
  497.3 3.9 copy-start
  516.5 3.9 copy-start
  535.7 3.9 copy-start
  547.9 12.2 %copy-start.8 = (f32[12,1024,64]{1,2,0:T(8,128)S(1)}, f32[12,1024,64]{1,2,0:T(8,128)}, u32[]{:S(2)}) copy-start(f32[12,1024,64]{1,2,0:T(8,128)} %get-tuple-element.173) | copy-start | bytes 9437188
  566.6 1.8 copy-start.2
  566.6 2.4 copy-start.16
  566.7 2.4 copy-start.23
  566.7 2.4 copy-start.29
  566.7 2.4 copy-start.31
  566.7 2.4 copy-start.33
  567.0 1.2 copy-start.11
  576.1 294.4 %reduce-scatter.9.cloned.1.call-start = ((), (), s32[]{:S(2)}) async-start(), calls=%async_computation.10 | async-start | bytes 10616832 | tf_op jit(solution)/shard_map/reduce_scatter | solution.py:320
  586.8 448.6 %reduce-scatter.11.cloned.1.call-start = ((), (), s32[]{:S(2)}) async-start(), calls=%async_computation.11 | async-start | bytes 10616832 | tf_op jit(solution)/shard_map/reduce_scatter | solution.py:322
  596.7 0.7 copy-start.34
  596.7 487.6 %all-reduce.24.cloned.1.call-start = ((), (), s32[]{:S(2)}) async-start(), calls=%async_computation.12 | async-start | bytes 3538944 | tf_op jit(solution)/shard_map/psum | solution.py:329
  624.2 3.1 copy-start.6
  631.4 2.9 copy-start.12
  1084.3 8.0 copy-start.17
Sparse Core Ops, SparseCore 0:
  10.2 67.9 all-gather.5
  80.3 39.9 all-gather.7
  122.6 78.0 all-gather.9
  202.7 77.6 all-gather.11
  312.5 68.1 reduce-scatter.6
  576.2 129.4 reduce-scatter.4
  709.3 161.1 reduce-scatter.8
  874.1 161.1 reduce-scatter.10
  1039.1 45.1 all-reduce.23
where the time goes:
time: 1140 us; the launch traced here: 1130 us
  waiting for transfers between devices  402 us (35%)
  matrix products  366 us (32%)
  blocking collectives  131 us (11%)
  other arithmetic  101 us (9%)
  local copies, waits for them, and re-layouts  62 us (5%)
  loops' own time  40.6 us (4%)
  between operations  29.2 us (3%)
    reduce_scatter x1, waiting for transfers between devices, shards(): lax.psum_scatter(fc1_weight_grad, 'fsdp', scatter_dimension=0, tiled=True)  163 us
    reduce_scatter x1, waiting for transfers between devices, shards(): lax.psum_scatter(fc2_weight_grad, 'fsdp', scatter_dimension=0, tiled=True)  163 us
    dot_general x40, matrix products, matmul_right_t(): lax.dot_general(left, right, (((1,), (1,)), ((), ())), preferred_element_...  145 us
    dot_general x28, matrix products, matmul(): return jnp.dot(left, right, preferred_element_type=jnp.float32)  132 us
    dot_general x28, matrix products, matmul_left_t(): lax.dot_general(left, right, (((0,), (0,)), ((), ())), preferred_element_...  89.3 us
    unnamed x2, blocking collectives  75.9 us
    psum x1, waiting for transfers between devices, shards(): lax.psum(pieces[2].astype(jnp.bfloat16), 'dp').astype(jnp.float32)  42.1 us
    another operation x1, loops' own time, attend_bin_back(): d_query, d_key, d_value = lax.map(one_head, jnp.arange(H, dtype=jnp.int32))  32.2 us
  transfers between devices with their start and end apart: 9, of which 5 were waited for; matrix products, arithmetic and copies ran while one was open for 42% of the time, Pallas kernels for 0%

commit v1 on v0

--- a/solution.py
+++ b/solution.py
@@ -1,3 +1,4 @@
+import functools
 import jax
 import jax.numpy as jnp
 from jax import lax
@@ -9,6 +10,24 @@
 norm_eps = 1e-06
 masked_score = -1e30
 inv_sqrt_two_pi = 0.3989422804014327
+
+
+def time_the_body(inp, chip_axis):
+    taken_in = jax.lax.axis_index(chip_axis)
+    mid_arr = jax.lax.axis_size(chip_axis)
+    u_next, x_now, shaped = (mid_arr, taken_in, inp.shape[0])
+    far_arr, earlier = (inp, 1)
+    while earlier < u_next:
+        block_list = []
+        for tick in range(u_next):
+            block_list.append((tick, (tick - earlier) % u_next))
+        field_out = jax.lax.ppermute(far_arr, chip_axis, block_list)
+        far_arr = jnp.concatenate([far_arr, field_out], 0)
+        earlier = 2 * earlier
+    return jnp.roll(far_arr, x_now * shaped, axis=0)
+
+
+convert_tails = functools.partial(time_the_body, chip_axis="fsdp")
 
 
 def matmul(left, right):
@@ -181,7 +200,7 @@
         lax.all_gather(ln2_bias, "fsdp", axis=0, tiled=True),
         lax.all_gather(fc1_weight, "fsdp", axis=0, tiled=True),
         lax.all_gather(fc1_bias, "fsdp", axis=0, tiled=True),
-        lax.all_gather(fc2_weight, "fsdp", axis=0, tiled=True),
+        convert_tails(fc2_weight),
         lax.all_gather(fc2_bias, "fsdp", axis=0, tiled=True),
         lax.all_gather(frequencies, "fsdp", axis=0, tiled=True),
     )

time: 1140 us -> 1240 us (1.088)
  waiting for transfers between devices: 402 us -> 484 us
  local copies, waits for them, and re-layouts: 62 us -> 77 us
    ppermute x0 -> x3, waiting for transfers between devices: none -> 251 us  [time_the_body(): field_out = jax.lax.ppermute(far_arr, chip_axis, block_list)]
    reduce_scatter x1, waiting for transfers between devices: 163 us -> 12.4 us  [shards(): lax.psum_scatter(fc1_weight_grad, 'fsdp', scatter_dimension=0, tiled=True)]
    reduce_scatter x1, waiting for transfers between devices: 18.9 us -> 0.01 us  [shards(): lax.psum_scatter(qkv_weight_grad, 'fsdp', scatter_dimension=0, tiled=True)]
    unnamed x113 -> x128, local copies, waits for them, and re-layouts: 28 us -> 39.4 us
  transfers between devices with their start and end apart: 9 -> 12, of which waited for: 5 -> 7; matrix products, arithmetic and copies ran while one was open for 42% -> 40% of each run, Pallas kernels for 0% -> 0%
where the time goes in v1:
time: 1240 us
  waiting for transfers between devices  484 us (39%)
  matrix products  369 us (30%)
  blocking collectives  130 us (10%)
  other arithmetic  101 us (8%)
  local copies, waits for them, and re-layouts  77 us (6%)
  loops' own time  40.6 us (3%)
  between operations  29.3 us (2%)
    ppermute x3, waiting for transfers between devices, time_the_body(): field_out = jax.lax.ppermute(far_arr, chip_axis, block_list)  251 us
    reduce_scatter x1, waiting for transfers between devices, shards(): lax.psum_scatter(fc2_weight_grad, 'fsdp', scatter_dimension=0, tiled=True)  163 us
    dot_general x40, matrix products, matmul_right_t(): lax.dot_general(left, right, (((1,), (1,)), ((), ())), preferred_element_...  147 us
    dot_general x28, matrix products, matmul(): return jnp.dot(left, right, preferred_element_type=jnp.float32)  131 us
    dot_general x28, matrix products, matmul_left_t(): lax.dot_general(left, right, (((0,), (0,)), ((), ())), preferred_element_...  91.2 us
    unnamed x2, blocking collectives  74.8 us
    psum x1, waiting for transfers between devices, shards(): lax.psum(pieces[2].astype(jnp.bfloat16), 'dp').astype(jnp.float32)  42.2 us
    unnamed x128, local copies, waits for them, and re-layouts  39.4 us
  transfers between devices with their start and end apart: 12, of which 7 were waited for; matrix products, arithmetic and copies ran while one was open for 40% of the time, Pallas kernels for 0%

profile of v1, /device:TPU:0, one launch (start us, length us, event | category | flops | bytes accessed | tf_op | source)
XLA Modules:
  0.0 1235.8 jit_solution(14556381745924785482)
XLA Ops:
  19.5 40.6 %all-reduce.19 = (bf16[768]{0:T(1024)(128)(2,1)S(1)}, bf16[2304]{0:T(1024)(128)(2,1)S(1)}, bf16[768]{0:T(1024)(128)(2,1)S(1)}, bf16[768]{0:T(1024)(128)(2,1)S(1)...) all-reduce(bf16[768]{0:T(1024)(128)(2,1)S(1)} %dynamic-update-slice, ...), channel_id=1, replica_groups=mesh['fsdp'=8,'dp'=4] {'fsdp'}, use_global_device_ids=true, to_apply=%add.3 | all-reduce | flops 7680 | bytes 30720
  62.9 26.9 %all-gather = bf16[8,1,384]{2,1,0:T(2,128)(2,1)S(1)} all-gather(bf16[1,1,384]{2,1,0:T(2,128)(2,1)S(1)} %reshape.697), channel_id=1, replica_groups=mesh['fsdp'=8,'dp'=4] {'fsdp'}, dimensions={0}, use_global_device_ids=true | all-gather | bytes 6912 | tf_op jit(solution)/shard_map/all_gather | solution.py:202
  91.9 6.3 convolution_add_fusion
  98.3 3.1 fusion.100
  102.7 3.6 copy.81
  106.3 3.5 copy.82
  109.9 10.8 fusion.92
  127.2 83.8 %while.48 = (s32[]{:T(128)}, bf16[12,1024,64]{1,2,0:T(8,128)(2,1)}, f32[12,1024]{1,0:T(8,128)S(1)}, s32[12]{0:T(128)S(1)}, bf16[1024,768]{1,0:T(8,128)(2,1)S(1)}...) while((s32[]{:T(128)}, bf16[12,1024,64]{1,2,0:T(8,128)(2,1)}, ...), condition=%wide.region_9.10_spmd.clone, body=%wide.region_6.9_spmd.clone.sunk | while | flops 283180032 | bytes 13559479 | solution.py:137
  173.2 2.8 fusion.141
  208.1 2.9 fusion.141
  211.1 3.9 fusion.103
  217.1 50.6 %fusion.44 = (bf16[1024,3072]{1,0:T(8,128)(2,1)}, f32[1024,3072]{1,0:T(8,128)}) fusion(f32[3072]{0:T(1024)S(1)} %bitcast.99, bf16[768,3072]{1,0:T(8,128)(2,1)} %all-gather.10.cloned.1.call-done, f32[1024,768]{0,1:T(8,128)} %copy-done.4, f32[768]{0:T(1024)S(1)} %convert_element_type.206, f32[768]{0:T(1024)S(1)} %convert_element_type.205, ...), kind=kOutput, calls=%fused_computation.50 | convolution fusion | flops 5043388416 | bytes 26765312 | tf_op jit(solution)/shard_map/dot_general | solution.py:34
  267.7 12.7 %all-gather.12.cloned.1.call-done = bf16[3072,768]{1,0:T(8,128)(2,1)} async-done(((bf16[384,768]{1,0:T(8,128)(2,1)}), bf16[3072,768]{1,0:T(8,128)(2,1)}) %all-gather.12.cloned.1.call-update) | async-done | bytes 4718608 | tf_op jit(solution)/shard_map/all_gather | solution.py:261
  280.5 11.9 convert_reduce_fusion
  292.4 6.7 fusion.105
  299.1 3.7 copy.87
  302.7 3.0 multiply_reduce_fusion.1
  312.6 4.5 convolution_convert_fusion
  317.1 233.1 %while.49 = (s32[]{:T(128)}, f32[12,1024,64]{1,2,0:T(8,128)}, f32[12,1024,64]{1,2,0:T(8,128)}, bf16[12,1024,64]{1,2,0:T(8,128)(2,1)}, s32[12]{0:T(128)S(1)}, /*i...) while((s32[]{:T(128)}, f32[12,1024,64]{1,2,0:T(8,128)}, ...), condition=%wide.region_16.17_spmd.clone, body=%wide.region_14.16_spmd.clone.sunk | while | flops 681704448 | bytes 50888476 | solution.py:162
  318.8 3.9 fusion.150
  324.7 3.9 multiply_reduce_fusion.22
  338.2 3.9 fusion.150
  344.1 3.9 multiply_reduce_fusion.22
  357.6 3.9 fusion.150
  363.5 4.1 multiply_reduce_fusion.22
  377.2 3.9 fusion.150
  383.1 3.9 multiply_reduce_fusion.22
  396.5 3.9 fusion.150
  402.4 3.9 multiply_reduce_fusion.22
  415.9 3.9 fusion.150
  421.7 3.9 multiply_reduce_fusion.22
  435.2 3.9 fusion.150
  441.1 3.9 multiply_reduce_fusion.22
  454.6 3.9 fusion.150
  460.4 3.9 multiply_reduce_fusion.22
  473.9 3.9 fusion.150
  479.8 3.9 multiply_reduce_fusion.22
  493.3 3.9 fusion.150
  499.2 3.9 multiply_reduce_fusion.22
  512.7 3.9 fusion.150
  518.6 3.9 multiply_reduce_fusion.22
  532.0 3.9 fusion.150
  537.9 3.9 multiply_reduce_fusion.22
  550.2 12.1 multiply_subtract_fusion
  564.7 6.4 multiply_reduce_fusion.7
  572.5 8.4 fusion.94
  581.2 10.5 fusion.98
  593.1 10.1 fusion.106
  605.7 26.2 %collective-permute-done = bf16[384,768]{1,0:T(8,128)(2,1)S(1)} collective-permute-done((bf16[384,768]{1,0:T(8,128)(2,1)S(1)}, bf16[384,768]{1,0:T(8,128)(2,1)S(1)}, u32[]{:S(2)}, u32[]{:S(2)}) %collective-permute-start) | collective-permute-done | bytes 589856 | tf_op jit(solution)/shard_map/ppermute | solution.py:24
  632.9 50.1 %collective-permute-done.1 = bf16[768,768]{1,0:T(8,128)(2,1)S(1)} collective-permute-done((bf16[768,768]{1,0:T(8,128)(2,1)S(1)}, bf16[768,768]{1,0:T(8,128)(2,1)S(1)}, u32[]{:S(2)}, u32[]{:S(2)}) %collective-permute-start.1) | collective-permute-done | bytes 1179680 | tf_op jit(solution)/shard_map/ppermute | solution.py:24
  692.8 174.8 %collective-permute-done.2 = bf16[1536,768]{1,0:T(8,128)(2,1)} collective-permute-done((bf16[1536,768]{1,0:T(8,128)(2,1)}, bf16[1536,768]{1,0:T(8,128)(2,1)}, u32[]{:S(2)}, u32[]{:S(2)}) %collective-permute-start.2) | collective-permute-done | bytes 2359328 | tf_op jit(solution)/shard_map/ppermute | solution.py:24
  867.6 3.3 constant_dynamic-update-slice_fusion.4
  873.7 3.4 constant_dynamic-update-slice_fusion
  877.3 8.5 fusion.104
  885.8 3.6 copy.90
  893.3 34.2 %all-reduce.18 = (bf16[768]{0:T(1024)(128)(2,1)S(1)}, bf16[768]{0:T(1024)(128)(2,1)S(1)}, bf16[2304]{0:T(1024)(128)(2,1)S(1)}, bf16[768]{0:T(1024)(128)(2,1)S(1)...) all-reduce(f32[768]{0:T(1024)S(1)} %get-tuple-element.365, ...), channel_id=2, replica_groups=mesh['fsdp'=8,'dp'=4] {'fsdp'}, use_global_device_ids=true, to_apply=%region_20.21.clone | all-reduce | flops 10752 | bytes 64512
  928.1 3.9 fusion.72
  933.6 9.1 add_convert_fusion
  944.4 6.1 all-reduce.20
  961.2 12.4 %reduce-scatter.9.cloned.1.call-done = f32[96,3072]{1,0:T(8,128)} async-done(((f32[768,3072]{1,0:T(8,128)}), f32[96,3072]{1,0:T(8,128)}) %reduce-scatter.9.cloned.1.call-update) | async-done | bytes 1179664 | tf_op jit(solution)/shard_map/reduce_scatter | solution.py:339
  975.8 162.7 %reduce-scatter.11.cloned.1.call-done = f32[384,768]{1,0:T(8,128)} async-done(((f32[3072,768]{1,0:T(8,128)}), f32[384,768]{1,0:T(8,128)}) %reduce-scatter.11.cloned.1.call-update) | async-done | bytes 1179664 | tf_op jit(solution)/shard_map/reduce_scatter | solution.py:341
  1145.3 42.2 %all-reduce.24.cloned.1.call-done = (bf16[96,2304]{1,0:T(8,128)(2,1)}, bf16[96,768]{1,0:T(8,128)(2,1)}, bf16[96,3072]{1,0:T(8,128)(2,1)}, bf16[384,768]{1,0:T(8,128)(2,1)}) async-done(((bf16[96,2304]{1,0:T(8,128)(2,1)}, bf16[96,768]{1,0:T(8,128)(2,1)}, bf16[96,3072]{1,0:T(8,128)(2,1)}, bf16[384,768]{1,0:T(8,128)(2,1)}), (bf16[96,2304]{1,0:T(8,128)(2,1)}, bf16[96,768]{1,0:T(8,128)(2,1)}, ...) | async-done | bytes 1769488 | tf_op jit(solution)/shard_map/psum | solution.py:348
  1192.5 2.9 multiply_reduce_fusion.9
  1203.6 21.9 %all-reduce.17 = (f32[]{:T(128)}, f32[]{:T(128)}) all-reduce(f32[]{:T(128)} %get-tuple-element.469, f32[]{:T(128)S(6)} %add.317), channel_id=1, replica_groups=mesh['fsdp'=8,'dp'=4] {'fsdp'}, use_global_device_ids=true, to_apply=%region_56.57 | all-reduce | flops 2 | bytes 16 | tf_op jit(solution)/shard_map/psum | solution.py:361
  (380 shorter events, 261.7 us)
Async XLA Ops:
  7.2 84.7 %all-gather.6.cloned.1.call-start = ((), (), s32[]{:S(2)}) async-start(), calls=%async_computation.4 | async-start | bytes 3981312 | tf_op jit(solution)/shard_map/all_gather | solution.py:195
  7.9 203.1 %all-gather.8.cloned.1.call-start = ((), (), s32[]{:S(2)}) async-start(), calls=%async_computation.5 | async-start | bytes 1327104 | tf_op jit(solution)/shard_map/all_gather | solution.py:197
  8.7 208.4 %all-gather.10.cloned.1.call-start = ((), (), s32[]{:S(2)}) async-start(), calls=%async_computation.6 | async-start | bytes 5308416 | tf_op jit(solution)/shard_map/all_gather | solution.py:201
  9.4 271.1 %all-gather.12.cloned.1.call-start = ((), (), s32[]{:S(2)}) async-start(), calls=%async_computation.7 | async-start | bytes 5308416 | tf_op jit(solution)/shard_map/all_gather | solution.py:261
  10.0 947.6 %reduce-scatter.7.cloned.1.call-start = ((), (), s32[]{:S(2)}) async-start(), calls=%async_computation.9 | async-start | bytes 2654208 | tf_op jit(solution)/shard_map/reduce_scatter | solution.py:335
  60.0 31.9 %copy-start.32 = (f32[768]{0:T(1024)}, f32[768]{0:T(1024)S(1)}, u32[]{:S(2)}) copy-start(f32[768]{0:T(1024)S(1)} %convert_element_type.194) | copy-start | bytes 9220
  60.0 31.9 %copy-start.36 = (f32[768]{0:T(1024)}, f32[768]{0:T(1024)S(1)}, u32[]{:S(2)}) copy-start(f32[768]{0:T(1024)S(1)} %convert_element_type.195) | copy-start | bytes 9220
  60.1 2.8 copy-start.39
  60.1 2.9 copy-start.40
  60.1 29.8 %copy-start.18 = (bf16[1024,768]{1,0:T(8,128)(2,1)S(1)}, bf16[1024,768]{1,0:T(8,128)(2,1)}, u32[]{:S(2)}) copy-start(bf16[1024,768]{1,0:T(8,128)(2,1)} %param.35) | copy-start | bytes 4718596
  61.9 149.1 %copy-start.1 = (bf16[1024,768]{0,1:T(8,128)(2,1)}, bf16[1024,768]{0,1:T(8,128)(2,1)S(1)}, u32[]{:S(2)}) copy-start(bf16[1024,768]{0,1:T(8,128)(2,1)S(1)} %copy.80) | copy-start | bytes 4718596
  62.2 36.0 %copy-start.26 = (f32[1024]{0:T(1024)}, f32[1024]{0:T(1024)S(1)}, u32[]{:S(2)}) copy-start(f32[1024]{0:T(1024)S(1)} %broadcast_multiply_fusion.5) | copy-start | bytes 12292
  62.7 35.6 %copy-start.34 = (f32[1024]{0:T(1024)}, f32[1024]{0:T(1024)S(1)}, u32[]{:S(2)}) copy-start(f32[1024]{0:T(1024)S(1)} %add_rsqrt_fusion.1) | copy-start | bytes 12292
  62.8 47.1 %copy-start.22 = (f32[12,32]{1,0:T(8,128)}, f32[12,32]{1,0:T(8,128)S(1)}, u32[]{:S(2)}) copy-start(f32[12,32]{1,0:T(8,128)S(1)} %slice.79) | copy-start | bytes 4612
  62.9 47.0 %copy-start.24 = (f32[12,32]{1,0:T(8,128)}, f32[12,32]{1,0:T(8,128)S(1)}, u32[]{:S(2)}) copy-start(f32[12,32]{1,0:T(8,128)S(1)} %slice.81) | copy-start | bytes 4612
  91.9 18.0 %copy-start.28 = (f32[1024]{0:T(1024)}, f32[1024]{0:T(1024)S(1)}, u32[]{:S(2)}) copy-start(f32[1024]{0:T(1024)S(1)} %get-tuple-element.490) | copy-start | bytes 12292
  91.9 18.0 %copy-start.30 = (f32[1024]{0:T(1024)}, f32[1024]{0:T(1024)S(1)}, u32[]{:S(2)}) copy-start(f32[1024]{0:T(1024)S(1)} %get-tuple-element.491) | copy-start | bytes 12292
  211.0 4.0 copy-start.11
  215.0 1.6 copy-start.4
  217.1 63.4 %copy-start.19 = (bf16[1024,768]{1,0:T(8,128)(2,1)S(1)}, bf16[1024,768]{1,0:T(8,128)(2,1)}, u32[]{:S(2)}) copy-start(bf16[1024,768]{1,0:T(8,128)(2,1)} %param.35) | copy-start | bytes 4718596
  280.5 11.9 copy-start.41
  292.4 6.7 copy-start.44
  299.1 3.7 copy-start.5
  302.7 3.1 copy-start.7
  302.7 3.3 copy-start.17
  306.0 3.4 copy-start.43
  309.5 3.1 copy-start.42
  312.3 646.9 %reduce-scatter.5.cloned.1.call-start = ((), (), s32[]{:S(2)}) async-start(), calls=%async_computation.8 | async-start | bytes 7962624 | tf_op jit(solution)/shard_map/reduce_scatter | solution.py:333
  317.0 233.1 %copy-start.3 = (f32[1024,768]{0,1:T(8,128)S(1)}, f32[1024,768]{0,1:T(8,128)}, u32[]{:S(2)}) copy-start(f32[1024,768]{0,1:T(8,128)} %copy.81) | copy-start | bytes 9437188
  317.0 233.1 %copy-start.23 = (f32[12,32]{1,0:T(8,128)S(1)}, f32[12,32]{1,0:T(8,128)}, u32[]{:S(2)}) copy-start(f32[12,32]{1,0:T(8,128)} %copy-done.22) | copy-start | bytes 4612
  317.0 233.1 %copy-start.25 = (f32[12,32]{1,0:T(8,128)S(1)}, f32[12,32]{1,0:T(8,128)}, u32[]{:S(2)}) copy-start(f32[12,32]{1,0:T(8,128)} %copy-done.24) | copy-start | bytes 4612
  317.0 233.1 %copy-start.29 = (f32[1024]{0:T(1024)S(1)}, f32[1024]{0:T(1024)}, u32[]{:S(2)}) copy-start(f32[1024]{0:T(1024)} %copy-done.28) | copy-start | bytes 12292
  317.1 233.1 %copy-start.31 = (f32[1024]{0:T(1024)S(1)}, f32[1024]{0:T(1024)}, u32[]{:S(2)}) copy-start(f32[1024]{0:T(1024)} %copy-done.30) | copy-start | bytes 12292
  324.7 3.9 copy-start
  344.1 3.9 copy-start
  363.5 4.1 copy-start
  383.0 3.9 copy-start
  402.4 3.9 copy-start
  421.7 3.9 copy-start
  441.1 3.9 copy-start
  460.4 3.9 copy-start
  479.8 3.9 copy-start
  499.2 3.9 copy-start
  518.6 3.9 copy-start
  537.9 3.9 copy-start
  562.2 2.5 copy-start.9
  562.4 8.9 copy-start.14
  564.7 7.7 copy-start.2
  564.7 7.7 copy-start.27
  564.7 7.7 copy-start.33
  564.7 7.7 copy-start.35
  564.7 7.7 copy-start.37
  580.9 392.7 %reduce-scatter.9.cloned.1.call-start = ((), (), s32[]{:S(2)}) async-start(), calls=%async_computation.10 | async-start | bytes 10616832 | tf_op jit(solution)/shard_map/reduce_scatter | solution.py:339
  591.7 546.7 %reduce-scatter.11.cloned.1.call-start = ((), (), s32[]{:S(2)}) async-start(), calls=%async_computation.11 | async-start | bytes 10616832 | tf_op jit(solution)/shard_map/reduce_scatter | solution.py:341
  603.3 85.6 %copy-start.38 = (bf16[768]{0:T(1024)(128)(2,1)S(1)}, bf16[768]{0:T(1024)(128)(2,1)}, u32[]{:S(2)}) copy-start(bf16[768]{0:T(1024)(128)(2,1)} %get-tuple-element.431) | copy-start | bytes 4612
  603.3 584.2 %all-reduce.24.cloned.1.call-start = ((), (), s32[]{:S(2)}) async-start(), calls=%async_computation.12 | async-start | bytes 3538944 | tf_op jit(solution)/shard_map/psum | solution.py:348
  604.3 27.5 %collective-permute-start = (bf16[384,768]{1,0:T(8,128)(2,1)S(1)}, bf16[384,768]{1,0:T(8,128)(2,1)S(1)}, u32[]{:S(2)}, u32[]{:S(2)}) collective-permute-start(bf16[384,768]{1,0:T(8,128)(2,1)S(1)} %copy-done.8), channel_id=1, source_target_pairs={{0,28},{4,0},{8,4},{12,8},{16,12},{20,16},{24,20},{28,24},{1,29},{... | collective-permute-start | bytes 1769480 | tf_op jit(solution)/shard_map/ppermute | solution.py:24
  631.8 52.7 %copy-start.12 = (bf16[384,768]{1,0:T(8,128)(2,1)}, bf16[384,768]{1,0:T(8,128)(2,1)S(1)}, u32[]{:S(2)}) copy-start(bf16[384,768]{1,0:T(8,128)(2,1)S(1)} %collective-permute-done) | copy-start | bytes 1769476
  631.9 51.1 %collective-permute-start.1 = (bf16[768,768]{1,0:T(8,128)(2,1)S(1)}, bf16[768,768]{1,0:T(8,128)(2,1)S(1)}, u32[]{:S(2)}, u32[]{:S(2)}) collective-permute-start(bf16[768,768]{1,0:T(8,128)(2,1)S(1)} %pad_maximum_fusion.6), channel_id=1, source_target_pairs={{0,24},{4,28},{8,0},{12,4},{16,8},{20,12},{24,16},{28,20},{1,25},{... | collective-permute-start | bytes 3538952 | tf_op jit(solution)/shard_map/ppermute | solution.py:24
  684.6 183.1 %collective-permute-start.2 = (bf16[1536,768]{1,0:T(8,128)(2,1)}, bf16[1536,768]{1,0:T(8,128)(2,1)}, u32[]{:S(2)}, u32[]{:S(2)}) collective-permute-start(bf16[1536,768]{1,0:T(8,128)(2,1)} %pad_maximum_fusion.1), channel_id=1, source_target_pairs={{0,16},{4,20},{8,24},{12,28},{16,0},{20,4},{24,8},{28,12},{1,17},{... | collective-permute-start | bytes 7077896 | tf_op jit(solution)/shard_map/ppermute | solution.py:24
  692.8 178.9 %copy-start.13 = (bf16[384,768]{1,0:T(8,128)(2,1)S(1)}, bf16[384,768]{1,0:T(8,128)(2,1)}, u32[]{:S(2)}) copy-start(bf16[384,768]{1,0:T(8,128)(2,1)} %copy-done.12) | copy-start | bytes 1769476
  873.7 3.5 copy-start.15
  889.3 2.9 copy-start.6
  1187.5 7.9 copy-start.21
  (4 other events, 5.2 us)
Sparse Core Ops, SparseCore 0:
  10.2 67.9 all-gather.5
  80.3 39.9 all-gather.7
  122.5 78.1 all-gather.9
  202.7 77.6 all-gather.11
  312.4 67.9 reduce-scatter.6
  581.0 201.8 reduce-scatter.4
  786.5 187.0 reduce-scatter.8
  977.2 161.2 reduce-scatter.10
  1142.2 45.2 all-reduce.23
